TPU v7x, 256 devices: a whole 4x4x8 slice. The times are simulated.
256 devices in a mesh: replica: 8 (over y, core), fsdp: 32 (over x, z).
Axes of the slice: x: 4, y: 4, z: 8, core: 2. Of those that a mesh axis runs over, the one named last changes fastest.
Arguments:
- anchor_params: bfloat16 [24, 512, 4096], P(None, 'fsdp')
- replica_params: bfloat16 [8, 24, 512, 4096], P('replica', None, 'fsdp')
- projection: bfloat16 [4096, 384], replicated
- momentum: float32 [24, 512, 384], P(None, 'fsdp'), may hold values from -1.8 to 1.8
- rate_table: float32 [4, 6], replicated, may hold values from 0.1 to 1
- owner_list: int32 [24], replicated, may hold values from 0 to 31, as said below
- layer_kind: int32 [24, 2], replicated, may hold values from 0 to 5, as said below
Outputs:
- new_params: bfloat16 [24, 512, 4096], P(None, 'fsdp')
- new_momentum: float32 [24, 512, 384], P(None, 'fsdp')
Inputs may be any that keep to these rules, and one draw needn't show every extreme that they name: `owner_list`: no fsdp index is named more than 2 times, and in every draw some index is named exactly 2 times. `layer_kind`: column 0 is a layer, column 1 a kind below 6; each layer has 6 rows, and no two rows are equal.
All inputs are finite; a program needn't handle non-finite values.
Results may differ from a plain program's by a relative error of at most 0.0055.
Values may be sent and summed in bfloat16 or wider, within the bound.
No kernel may reach another device: no remote copies, remote signals or barrier semaphores. Data moves between devices by JAX's collectives and lax.ppermute only.
A program may use at most 128 MiB of HBM per device.

v0:
```python
import jax
import jax.numpy as jnp
from jax import lax
from jax.sharding import PartitionSpec as P

OUTER_MOMENTUM = 0.9
EPSILON = 1e-06


def local(anchor_params, replica_params, projection, momentum, rate_table, owner_list, layer_kind):
    matrices, rows_dev, model_width = anchor_params.shape
    rank_dim = projection.shape[1]
    all_rows = rows_dev * lax.axis_size("fsdp")
    highest = lax.Precision.HIGHEST
    pseudo_grad = (
        anchor_params.astype(jnp.float32) - replica_params[0].astype(jnp.float32)
    ).astype(jnp.bfloat16)
    compressed = jnp.dot(
        pseudo_grad.reshape(matrices * rows_dev, model_width),
        projection,
        preferred_element_type=jnp.float32,
    )
    summed = lax.psum(compressed.reshape(matrices, rows_dev, rank_dim), "replica")
    outer_grad = summed / lax.axis_size("replica")
    new_momentum = OUTER_MOMENTUM * momentum + outer_grad
    outer_step = outer_grad + OUTER_MOMENTUM * new_momentum
    squares = lax.psum(jnp.sum(outer_step * outer_step, axis=(1, 2)), "fsdp")
    same_group = (owner_list[:, None] == owner_list[None, :]).astype(jnp.float32)
    group_squares = jnp.dot(same_group, squares, precision=highest)
    group_count = jnp.sum(same_group, axis=1)
    scaling = lax.rsqrt(group_squares / (group_count * (all_rows * rank_dim)) + EPSILON)
    outer_rate = rate_table[layer_kind[:, 0], layer_kind[:, 1]]
    direction = (outer_step * (outer_rate * scaling)[:, None, None]).astype(jnp.bfloat16)
    update = lax.dot_general(
        direction.reshape(matrices * rows_dev, rank_dim),
        projection,
        (((1,), (1,)), ((), ())),
        preferred_element_type=jnp.float32,
    ).astype(jnp.bfloat16)
    new_params = (
        anchor_params.astype(jnp.float32)
        - update.reshape(matrices, rows_dev, model_width).astype(jnp.float32)
    ).astype(jnp.bfloat16)
    return (new_params, new_momentum)


def solution(mesh):
    placed = (
        P(None, "fsdp", None),
        P("replica", None, "fsdp", None),
        P(),
        P(None, "fsdp", None),
        P(),
        P(),
        P(),
    )
    return jax.shard_map(
        local,
        mesh=mesh,
        in_specs=placed,
        out_specs=(P(None, "fsdp", None), P(None, "fsdp", None)),
        check_vma=False,
    )
```

profile of v0, /device:TPU:0, one launch (start us, length us, event | category | flops | bytes accessed | tf_op | source)
XLA Modules:
  0.0 172.9 jit_solution(15849342084656338026)
XLA Ops:
  7.2 0.0 copy-start
  7.2 0.0 copy-start.3
  7.2 0.0 copy-start.1
  7.2 0.0 copy-start.4
  7.2 0.0 all-reduce.2.cloned.1.call-start
  7.3 1.8 %copy-done = bf16[4096,384]{1,0:T(8,128)(2,1)S(1)} copy-done((bf16[4096,384]{1,0:T(8,128)(2,1)S(1)}, bf16[4096,384]{1,0:T(8,128)(2,1)}, u32[]{:S(2)}) %copy-start) | copy-done | bytes 3145752
  9.1 5.5 %fusion.2 = f32[24,16,384]{2,1,0:T(8,128)} fusion(bf16[24,16,4096]{2,1,0:T(8,128)(2,1)} %param.7, bf16[1,24,16,4096]{3,2,1,0:T(8,128)(2,1)} %param.8, bf16[4096,384]{1,0:T(8,128)(2,1)S(1)} %copy-done), kind=kOutput, calls=%fused_computation.6 | convolution fusion | flops 1214251008 | bytes 10027008 | tf_op jit(solution)/shard_map/dot_general | solution.py:18
  14.5 0.0 all-reduce.2.cloned.1.call-update
  14.5 0.0 copy-done.3
  14.6 0.0 copy-done.1
  14.6 0.8 gather_fusion
  15.4 0.0 copy-done.4
  15.4 0.2 fusion.11
  15.6 66.8 %all-reduce.2.cloned.1.call-done = f32[24,16,384]{2,1,0:T(8,128)} async-done(((f32[24,16,384]{2,1,0:T(8,128)}), f32[24,16,384]{2,1,0:T(8,128)}) %all-reduce.2.cloned.1.call-update) | async-done | bytes 589840 | tf_op jit(solution)/shard_map/psum | solution.py:23
  82.4 2.2 %multiply_reduce_fusion = (f32[24]{0:T(128)S(1)}, f32[24,16,384]{2,1,0:T(8,128)}) fusion(f32[24,16,384]{2,1,0:T(8,128)} %all-reduce.2.cloned.1.call-done, f32[24,16,384]{2,1,0:T(8,128)} %param.10), kind=kLoop, calls=%fused_computation.15 | loop fusion | flops 1032168 | bytes 1769568 | tf_op jit(solution)/shard_map/reduce_sum | solution.py:27
  84.7 75.0 %psum.15 = f32[24]{0:T(128)S(1)} all-reduce(f32[24]{0:T(128)S(1)} %get-tuple-element.2), channel_id=1, replica_groups=mesh['replica'=8,'fsdp'=32] {'fsdp'}, use_global_device_ids=true, to_apply=%region_2.0 | all-reduce | flops 24 | bytes 192 | tf_op jit(solution)/shard_map/psum | solution.py:27
  159.7 0.2 fusion.9
  159.9 1.4 multiply_convert_fusion
  161.3 0.0 copy-start.2
  161.3 1.8 %convolution_convert_fusion = bf16[384,4096]{1,0:T(8,128)(2,1)S(1)} fusion(bf16[384,384]{1,0:T(8,128)(2,1)S(1)} %bitcast.30, bf16[4096,384]{1,0:T(8,128)(2,1)S(1)} %copy-done), kind=kOutput, calls=%fused_computation.5 | convolution fusion | flops 1209532416 | bytes 6586368 | tf_op jit(solution)/shard_map/dot_general | solution.py:34
  163.1 0.0 copy-done.2
  163.2 2.9 %fusion.1 = bf16[24,16,4096]{2,1,0:T(8,128)(2,1)} fusion(bf16[24,16,4096]{2,1,0:T(8,128)(2,1)S(1)} %copy-done.2, bf16[24,16,4096]{2,1,0:T(8,128)(2,1)S(1)} %bitcast.29), kind=kLoop, calls=%fused_computation.4 | loop fusion | flops 6291456 | bytes 9437184 | tf_op jit(solution)/shard_map/convert_element_type | solution.py:43
  (1 shorter events, 0.0 us)
Async XLA Ops:
  7.2 1.9 %copy-start = (bf16[4096,384]{1,0:T(8,128)(2,1)S(1)}, bf16[4096,384]{1,0:T(8,128)(2,1)}, u32[]{:S(2)}) copy-start(bf16[4096,384]{1,0:T(8,128)(2,1)} %param.9) | copy-start | bytes 9437188
  7.2 7.4 %copy-start.3 = (s32[24,2]{0,1:T(2,128)S(1)}, s32[24,2]{0,1:T(2,128)}, u32[]{:S(2)}) copy-start(s32[24,2]{0,1:T(2,128)} %param.13) | copy-start | bytes 580
  7.2 7.4 %copy-start.1 = (f32[4,6]{1,0:T(4,128)S(1)}, f32[4,6]{1,0:T(4,128)}, u32[]{:S(2)}) copy-start(f32[4,6]{1,0:T(4,128)} %param.11) | copy-start | bytes 292
  7.2 8.2 %copy-start.4 = (s32[24]{0:T(128)S(1)}, s32[24]{0:T(128)}, u32[]{:S(2)}) copy-start(s32[24]{0:T(128)} %param.12) | copy-start | bytes 292
  7.2 75.2 %all-reduce.2.cloned.1.call-start = ((), (), s32[]{:S(2)}) async-start(), calls=%async_computation | async-start | bytes 1179648 | tf_op jit(solution)/shard_map/psum | solution.py:23
  161.3 1.9 %copy-start.2 = (bf16[24,16,4096]{2,1,0:T(8,128)(2,1)S(1)}, bf16[24,16,4096]{2,1,0:T(8,128)(2,1)}, u32[]{:S(2)}) copy-start(bf16[24,16,4096]{2,1,0:T(8,128)(2,1)} %param.7) | copy-start | bytes 9437188
Sparse Core Ops, SparseCore 0:
  14.7 67.7 all-reduce.1
where the time goes:
time: 173 us
  blocking collectives  75 us (43%)
  waiting for transfers between devices  66.8 us (39%)
  between operations  14.1 us (8%)
  matrix products  7.48 us (4%)
  other arithmetic  6.67 us (4%)
  local copies, waits for them, and re-layouts  2.71 us (2%)
    psum x1, blocking collectives, local(): squares = lax.psum(jnp.sum(outer_step * outer_step, axis=(1, 2)), 'fsdp')  75 us
    psum x1, waiting for transfers between devices, local(): lax.psum(compressed.reshape(matrices, rows_dev, rank_dim), 'replica')  66.8 us
    dot_general x1, matrix products, local(): jnp.dot(pseudo_grad.reshape(matrices * rows_dev, model_width), projection...  5.45 us
  transfers between devices with their start and end apart: 1, of which 1 were waited for; matrix products, arithmetic and copies ran while one was open for 1% of the time, Pallas kernels for 0%

commit v1 on v0

--- a/solution.py
+++ b/solution.py
@@ -5,6 +5,12 @@
 
 OUTER_MOMENTUM = 0.9
 EPSILON = 1e-06
+
+
+def summed_here(x, name):
+    parts = lax.all_gather(x, name, axis=0, tiled=False)
+    result = parts.sum(axis=0)
+    return result
 
 
 def local(anchor_params, replica_params, projection, momentum, rate_table, owner_list, layer_kind):
@@ -20,7 +26,7 @@
         projection,
         preferred_element_type=jnp.float32,
     )
-    summed = lax.psum(compressed.reshape(matrices, rows_dev, rank_dim), "replica")
+    summed = summed_here(compressed.reshape(matrices, rows_dev, rank_dim), "replica")
     outer_grad = summed / lax.axis_size("replica")
     new_momentum = OUTER_MOMENTUM * momentum + outer_grad
     outer_step = outer_grad + OUTER_MOMENTUM * new_momentum

time: 173 us -> 148 us (0.86)
  waiting for transfers between devices: 66.8 us -> 37.2 us
  other arithmetic: 6.67 us -> 10.2 us
    psum x1 -> x0, waiting for transfers between devices: 66.8 us -> none  [local(): lax.psum(compressed.reshape(matrices, rows_dev, rank_dim), 'replica')]
    all_gather x0 -> x1, waiting for transfers between devices: none -> 37.2 us  [summed_here(): parts = lax.all_gather(x, name, axis=0, tiled=False)]
    reduce_sum x0 -> x1, other arithmetic: none -> 3.51 us  [summed_here(): result = parts.sum(axis=0)]
where the time goes in v1:
time: 148 us; the launch traced here: 147 us
  blocking collectives  75 us (51%)
  waiting for transfers between devices  37.2 us (25%)
  between operations  14.1 us (10%)
  other arithmetic  10.2 us (7%)
  matrix products  7.48 us (5%)
  local copies, waits for them, and re-layouts  2.71 us (2%)
    psum x1, blocking collectives, local(): squares = lax.psum(jnp.sum(outer_step * outer_step, axis=(1, 2)), 'fsdp')  75 us
    all_gather x1, waiting for transfers between devices, summed_here(): parts = lax.all_gather(x, name, axis=0, tiled=False)  37.2 us
    dot_general x1, matrix products, local(): jnp.dot(pseudo_grad.reshape(matrices * rows_dev, model_width), projection...  5.45 us
    reduce_sum x1, other arithmetic, summed_here(): result = parts.sum(axis=0)  3.51 us
  transfers between devices with their start and end apart: 1, of which 1 were waited for; matrix products, arithmetic and copies ran while one was open for 1% of the time, Pallas kernels for 0%

profile of v1, /device:TPU:0, one launch (start us, length us, event | category | flops | bytes accessed | tf_op | source)
XLA Modules:
  0.0 146.8 jit_solution(14506026319293707249)
XLA Ops:
  7.2 0.0 copy-start
  7.2 0.0 copy-start.3
  7.2 0.0 copy-start.1
  7.2 0.0 copy-start.4
  7.2 0.0 all-gather.3.cloned.1.call-start
  7.3 1.8 %copy-done = bf16[4096,384]{1,0:T(8,128)(2,1)S(1)} copy-done((bf16[4096,384]{1,0:T(8,128)(2,1)S(1)}, bf16[4096,384]{1,0:T(8,128)(2,1)}, u32[]{:S(2)}) %copy-start) | copy-done | bytes 3145752
  9.1 5.5 %fusion.2 = f32[24,16,384]{2,1,0:T(8,128)} fusion(bf16[24,16,4096]{2,1,0:T(8,128)(2,1)} %param.7, bf16[1,24,16,4096]{3,2,1,0:T(8,128)(2,1)} %param.8, bf16[4096,384]{1,0:T(8,128)(2,1)S(1)} %copy-done), kind=kOutput, calls=%fused_computation.6 | convolution fusion | flops 1214251008 | bytes 10027008 | tf_op jit(solution)/shard_map/dot_general | solution.py:24
  14.5 0.0 all-gather.3.cloned.1.call-update
  14.5 0.0 copy-done.3
  14.6 0.0 copy-done.1
  14.6 0.8 gather_fusion
  15.4 0.0 copy-done.4
  15.4 0.2 fusion.11
  15.6 37.2 %all-gather.3.cloned.1.call-done = f32[192,16,384]{2,1,0:T(8,128)} async-done(((f32[24,16,384]{2,1,0:T(8,128)}), f32[192,16,384]{2,1,0:T(8,128)}) %all-gather.3.cloned.1.call-update) | async-done | bytes 4718608 | tf_op jit(solution)/shard_map/all_gather | solution.py:11
  52.8 3.5 %reduce_sum.27 = f32[24,16,384]{2,1,0:T(8,128)} reduce(f32[8,24,16,384]{3,2,1,0:T(8,128)} %bitcast.30, f32[]{:T(128)} %constant.1.clone.1), dimensions={0}, to_apply=%region_0.0 | reduce | flops 1032192 | bytes 5308420 | tf_op jit(solution)/shard_map/reduce_sum | solution.py:12
  56.3 2.2 %multiply_reduce_fusion = (f32[24]{0:T(128)S(1)}, f32[24,16,384]{2,1,0:T(8,128)}) fusion(f32[24,16,384]{2,1,0:T(8,128)} %reduce_sum.27, f32[24,16,384]{2,1,0:T(8,128)} %param.10), kind=kLoop, calls=%fused_computation.15 | loop fusion | flops 1032168 | bytes 1769568 | tf_op jit(solution)/shard_map/reduce_sum | solution.py:33
  58.5 75.0 %psum.7 = f32[24]{0:T(128)S(1)} all-reduce(f32[24]{0:T(128)S(1)} %get-tuple-element.2), channel_id=1, replica_groups=mesh['replica'=8,'fsdp'=32] {'fsdp'}, use_global_device_ids=true, to_apply=%region_2.0 | all-reduce | flops 24 | bytes 192 | tf_op jit(solution)/shard_map/psum | solution.py:33
  133.6 0.2 fusion.9
  133.8 1.4 multiply_convert_fusion
  135.1 0.0 copy-start.2
  135.2 1.8 %convolution_convert_fusion = bf16[384,4096]{1,0:T(8,128)(2,1)S(1)} fusion(bf16[384,384]{1,0:T(8,128)(2,1)S(1)} %bitcast.32, bf16[4096,384]{1,0:T(8,128)(2,1)S(1)} %copy-done), kind=kOutput, calls=%fused_computation.5 | convolution fusion | flops 1209532416 | bytes 6586368 | tf_op jit(solution)/shard_map/dot_general | solution.py:40
  137.0 0.0 copy-done.2
  137.0 2.9 %fusion.1 = bf16[24,16,4096]{2,1,0:T(8,128)(2,1)} fusion(bf16[24,16,4096]{2,1,0:T(8,128)(2,1)S(1)} %copy-done.2, bf16[24,16,4096]{2,1,0:T(8,128)(2,1)S(1)} %bitcast.31), kind=kLoop, calls=%fused_computation.4 | loop fusion | flops 6291456 | bytes 9437184 | tf_op jit(solution)/shard_map/convert_element_type | solution.py:49
  (1 shorter events, 0.0 us)
Async XLA Ops:
  7.2 1.9 %copy-start = (bf16[4096,384]{1,0:T(8,128)(2,1)S(1)}, bf16[4096,384]{1,0:T(8,128)(2,1)}, u32[]{:S(2)}) copy-start(bf16[4096,384]{1,0:T(8,128)(2,1)} %param.9) | copy-start | bytes 9437188
  7.2 7.4 %copy-start.3 = (s32[24,2]{0,1:T(2,128)S(1)}, s32[24,2]{0,1:T(2,128)}, u32[]{:S(2)}) copy-start(s32[24,2]{0,1:T(2,128)} %param.13) | copy-start | bytes 580
  7.2 7.4 %copy-start.1 = (f32[4,6]{1,0:T(4,128)S(1)}, f32[4,6]{1,0:T(4,128)}, u32[]{:S(2)}) copy-start(f32[4,6]{1,0:T(4,128)} %param.11) | copy-start | bytes 292
  7.2 8.2 %copy-start.4 = (s32[24]{0:T(128)S(1)}, s32[24]{0:T(128)}, u32[]{:S(2)}) copy-start(s32[24]{0:T(128)} %param.12) | copy-start | bytes 292
  7.2 45.6 %all-gather.3.cloned.1.call-start = ((), (), s32[]{:S(2)}) async-start(), calls=%async_computation | async-start | bytes 5308416 | tf_op jit(solution)/shard_map/all_gather | solution.py:11
  135.1 1.9 %copy-start.2 = (bf16[24,16,4096]{2,1,0:T(8,128)(2,1)S(1)}, bf16[24,16,4096]{2,1,0:T(8,128)(2,1)}, u32[]{:S(2)}) copy-start(bf16[24,16,4096]{2,1,0:T(8,128)(2,1)} %param.7) | copy-start | bytes 9437188
Sparse Core Ops, SparseCore 0:
  14.7 38.0 all-gather.2
